TPU v7x, 32 devices: a whole 2x2x4 slice. The times are simulated.
32 devices in a mesh: crop: 8 (over z, y), head: 4 (over x, core).
Axes of the slice: x: 2, y: 2, z: 4, core: 2. Of those that a mesh axis runs over, the one named last changes fastest.
Arguments:
- global_rows: bfloat16 [4096, 4096], P('crop', 'head'), may hold values from -6 to 6
- crop_tokens: bfloat16 [8192, 4096], P('crop', 'head'), may hold values from -6 to 6
- query_weight: bfloat16 [4096, 4096], P('crop', 'head'), may hold values from -0.125 to 0.125
- key_weight: bfloat16 [4096, 4096], P('crop', 'head'), may hold values from -0.125 to 0.125
- value_weight: bfloat16 [4096, 4096], P('crop', 'head'), may hold values from -0.09375 to 0.09375
- fetch_slots: int32 [8, 8, 2], P('crop'), may hold values from 0 to 63
- region_slots: int32 [128, 8], P('crop'), may hold values from 0 to 15, as said below
- region_len: int32 [128], P('crop'), may hold values from 4 to 8
Outputs:
- attended: bfloat16 [4096, 4096], P('crop', 'head')
Inputs may be any that keep to these rules, and one draw needn't show every extreme that they name: `fetch_slots`: entry [s, o, c] numbers one of the 64 crop blocks of index s of crop. `region_slots`: the blocks listed for one page-row are distinct; the lists of the 16 page-rows of one index of crop together name all 16 delivered blocks. page-row r uses its first region_len[r] listed blocks.
All inputs are finite; a program needn't handle non-finite values.
Results may differ from a plain program's by a relative error of at most 0.008.
Values may be sent and summed in bfloat16 or wider, within the bound.
No kernel may reach another device: no remote copies, remote signals or barrier semaphores. Data moves between devices by JAX's collectives and lax.ppermute only.
A program may use at most 128 MiB of HBM per device.

v0:
```python
import jax
import jax.numpy as jnp
from jax import lax
from jax.sharding import PartitionSpec as P

HD = 128
CT = 16
CAP = 2
NB = 8
GR = 32


def add_rows(left, piece):
    return jnp.dot(left, piece, preferred_element_type=jnp.float32)


def body(
    global_rows,
    crop_tokens,
    query_weight,
    key_weight,
    value_weight,
    fetch_slots,
    region_slots,
    region_len,
):
    width = key_weight.shape[1]
    heads_here = width // HD
    ncrop = lax.axis_size("crop")
    rows_here = region_slots.shape[0]
    queries_in = lax.all_gather(global_rows, "head", axis=1, tiled=True)
    query = add_rows(queries_in, lax.all_gather(query_weight, "crop", axis=0, tiled=True)).astype(
        jnp.bfloat16
    )
    picks = fetch_slots[0]
    tokens_all = lax.all_gather(crop_tokens, "head", axis=1, tiled=True)

    def add_one(piece):
        return add_rows(tokens_all, piece)

    keys_full = add_one(lax.all_gather(key_weight, "crop", axis=0, tiled=True))
    vals_full = add_one(lax.all_gather(value_weight, "crop", axis=0, tiled=True))
    packed = jnp.concatenate(
        [keys_full.astype(jnp.bfloat16), vals_full.astype(jnp.bfloat16)], axis=1
    )
    packed = packed.reshape(-1, CT, 2 * width)
    outgoing = packed[picks]
    incoming = lax.all_to_all(outgoing, "crop", split_axis=0, concat_axis=0, tiled=True)
    slotted = incoming.reshape(ncrop * CAP, CT, 2 * width)
    listed = slotted[region_slots].reshape(rows_here, NB * CT, 2 * width)
    keys_row = listed[:, :, :width].reshape(rows_here, NB * CT, heads_here, HD)
    vals_row = listed[:, :, width:].reshape(rows_here, NB * CT, heads_here, HD)
    query_row = query.reshape(rows_here, GR, heads_here, HD)
    scale = 1.0 / HD**0.5
    scores = (
        jnp.einsum("rghe,rkhe->rhgk", query_row, keys_row, preferred_element_type=jnp.float32)
        * scale
    )
    used = (jnp.arange(NB * CT, dtype=jnp.int32) // CT)[None, :] < region_len[:, None]
    scores = jnp.where(used[:, None, None, :], scores, jnp.float32(-1e30))
    top = jnp.max(scores, axis=-1, keepdims=True)
    expo = jnp.exp(scores - top)
    weights = (expo / jnp.sum(expo, axis=-1, keepdims=True)).astype(jnp.bfloat16)
    result = jnp.einsum("rhgk,rkhe->rghe", weights, vals_row, preferred_element_type=jnp.float32)
    return result.astype(jnp.bfloat16).reshape(rows_here * GR, width)


def solution(mesh):
    placed = (
        P("crop", "head"),
        P("crop", "head"),
        P("crop", "head"),
        P("crop", "head"),
        P("crop", "head"),
        P("crop", None, None),
        P("crop", None),
        P("crop"),
    )
    return jax.shard_map(
        body, mesh=mesh, in_specs=placed, out_specs=P("crop", "head"), check_vma=False
    )
```

profile of v0, /device:TPU:0, one launch (start us, length us, event | category | flops | bytes accessed | tf_op | source)
XLA Modules:
  0.0 549.0 jit_solution(13589215673044014440)
XLA Ops:
  6.5 0.7 all-gather.6.cloned.1.call-update
  7.3 0.7 all-gather.8.cloned.1.call-update
  8.1 0.7 all-gather.10.cloned.1.call-update
  10.3 59.6 %all-gather.6.cloned.1.call-done = bf16[1024,4096]{1,0:T(8,128)(2,1)} async-done(((bf16[1024,1024]{1,0:T(8,128)(2,1)}), bf16[1024,4096]{1,0:T(8,128)(2,1)}) %all-gather.6.cloned.1.call-update) | async-done | bytes 8388624 | tf_op jit(solution)/shard_map/all_gather | solution.py:36
  69.9 127.1 %all-gather.8.cloned.1.call-done = bf16[4096,1024]{1,0:T(8,128)(2,1)} async-done(((bf16[512,1024]{1,0:T(8,128)(2,1)}), bf16[4096,1024]{1,0:T(8,128)(2,1)}) %all-gather.8.cloned.1.call-update) | async-done | bytes 8388624 | tf_op jit(solution)/shard_map/all_gather | solution.py:41
  197.0 13.7 %convolution_convert_fusion.1 = bf16[1024,1024]{0,1:T(8,128)(2,1)S(1)} fusion(bf16[1024,4096]{1,0:T(8,128)(2,1)} %all-gather.6.cloned.1.call-done, bf16[4096,1024]{1,0:T(8,128)(2,1)} %all-gather.8.cloned.1.call-done), kind=kOutput, calls=%fused_computation.8 | convolution fusion | flops 8590983168 | bytes 18874368 | tf_op jit(solution)/shard_map/dot_general | solution.py:14
  210.8 111.5 %all-gather.10.cloned.1.call-done = bf16[4096,1024]{1,0:T(8,128)(2,1)} async-done(((bf16[512,1024]{1,0:T(8,128)(2,1)}), bf16[4096,1024]{1,0:T(8,128)(2,1)}) %all-gather.10.cloned.1.call-update) | async-done | bytes 8388624 | tf_op jit(solution)/shard_map/all_gather | solution.py:42
  322.3 13.7 %convolution_convert_fusion = bf16[1024,1024]{0,1:T(8,128)(2,1)S(1)} fusion(bf16[1024,4096]{1,0:T(8,128)(2,1)} %all-gather.6.cloned.1.call-done, bf16[4096,1024]{1,0:T(8,128)(2,1)} %all-gather.10.cloned.1.call-done), kind=kOutput, calls=%fused_computation.7 | convolution fusion | flops 8590983168 | bytes 18874368 | tf_op jit(solution)/shard_map/dot_general | solution.py:14
  336.1 2.4 pad_maximum_fusion
  338.5 6.6 %copy.12 = bf16[1024,2048]{1,0:T(8,128)(2,1)} copy(bf16[1024,2048]{0,1:T(8,128)(2,1)} %pad_maximum_fusion) | data formatting | bytes 8388608 | tf_op jit(solution)/shard_map/concatenate | solution.py:43
  345.1 3.8 gather_fusion
  348.9 3.7 all-to-all-start
  352.7 3.7 all-gather.12.cloned.1.call-done
  356.4 133.9 %all-gather.14.cloned.1.call-done = bf16[4096,1024]{1,0:T(8,128)(2,1)} async-done(((bf16[512,1024]{1,0:T(8,128)(2,1)}), bf16[4096,1024]{1,0:T(8,128)(2,1)}) %all-gather.14.cloned.1.call-update) | async-done | bytes 8388624 | tf_op jit(solution)/shard_map/all_gather | solution.py:32
  490.3 9.1 %fusion.3 = bf16[64,8,8,128]{3,1,2,0:T(8,128)(2,1)S(1)} fusion(bf16[512,4096]{1,0:T(8,128)(2,1)} %all-gather.12.cloned.1.call-done, bf16[4096,1024]{1,0:T(8,128)(2,1)} %all-gather.14.cloned.1.call-done), kind=kOutput, calls=%fused_computation.13 | convolution fusion | flops 4295491584 | bytes 13631488 | tf_op jit(solution)/shard_map/dot_general | solution.py:14
  499.7 6.2 %gather_fusion.1 = bf16[128,16,2048]{2,1,0:T(8,128)(2,1)} fusion(bf16[16,16,2048]{2,1,0:T(8,128)(2,1)S(1)} %bitcast.29, s32[1024]{0:T(1024)S(1)} %pad_clamp_fusion), kind=kCustom, calls=%fused_computation.1 | custom fusion | bytes 16777728 | tf_op jit(solution)/shard_map/gather | solution.py:50
  506.0 6.0 %fusion.17 = (bf16[16,128,1024]{2,1,0:T(8,128)(2,1)}, bf16[16,128,1024]{2,1,0:T(8,128)(2,1)}) fusion(bf16[16,128,2048]{2,1,0:T(8,128)(2,1)} %bitcast.30), kind=kLoop, calls=%fused_computation.35 | loop fusion | bytes 16777216 | tf_op jit(solution)/shard_map/slice | solution.py:51
  512.0 6.4 %copy.16 = bf16[16,128,1024]{1,2,0:T(8,128)(2,1)} copy(bf16[16,128,1024]{2,1,0:T(8,128)(2,1)} %get-tuple-element.5) | data formatting | bytes 8388608 | tf_op jit(solution)/shard_map/slice | solution.py:51
  518.4 6.4 %copy.15 = bf16[16,128,1024]{1,2,0:T(8,128)(2,1)} copy(bf16[16,128,1024]{2,1,0:T(8,128)(2,1)} %get-tuple-element.6) | data formatting | bytes 8388608 | tf_op jit(solution)/shard_map/slice | solution.py:52
  524.8 3.4 fusion.4
  528.2 1.3 copy-done
  529.5 1.2 fusion.18
  530.7 10.1 %fusion.2 = bf16[16,32,8,128]{3,1,2,0:T(8,128)(2,1)S(1)} fusion(bf16[16,128,8,128]{1,3,2,0:T(8,128)(2,1)} %bitcast.34, f32[16,8,32]{2,1,0:T(8,128)S(1)} %fusion.18, f32[16,8,32,128]{3,2,1,0:T(8,128)} %copy-done, pred[16,128]{1,0:T(8,128)(4,1)S(1)} %broadcast_compare_fusion), kind=kOutput, calls=%fused_computation.12 | convolution fusion | flops 137367680 | bytes 7358464 | tf_op jit(solution)/shard_map/rhgk,rkhe->rghe/dot_general | solution.py:64
  541.2 1.2 copy.28
  (27 shorter events, 2.4 us)
Async XLA Ops:
  6.5 3.4 copy-start.2
  6.5 3.6 copy-start.1
  6.5 63.4 %all-gather.6.cloned.1.call-start = ((), (), s32[]{:S(2)}) async-start(), calls=%async_computation.1 | async-start | bytes 10485760 | tf_op jit(solution)/shard_map/all_gather | solution.py:36
  7.3 189.8 %all-gather.8.cloned.1.call-start = ((), (), s32[]{:S(2)}) async-start(), calls=%async_computation.2 | async-start | bytes 9437184 | tf_op jit(solution)/shard_map/all_gather | solution.py:41
  8.0 314.3 %all-gather.10.cloned.1.call-start = ((), (), s32[]{:S(2)}) async-start(), calls=%async_computation.3 | async-start | bytes 9437184 | tf_op jit(solution)/shard_map/all_gather | solution.py:42
  8.7 347.7 %all-gather.12.cloned.1.call-start = ((), (), s32[]{:S(2)}) async-start(), calls=%async_computation.4 | async-start | bytes 5242880 | tf_op jit(solution)/shard_map/all_gather | solution.py:31
  9.3 481.0 %all-gather.14.cloned.1.call-start = ((), (), s32[]{:S(2)}) async-start(), calls=%async_computation.5 | async-start | bytes 9437184 | tf_op jit(solution)/shard_map/all_gather | solution.py:32
  345.1 7.5 %copy-start.3 = (s32[16]{0:T(128)S(1)}, s32[16]{0:T(128)}, u32[]{:S(2)}) copy-start(s32[16]{0:T(128)} %param.15) | copy-start | bytes 196
  348.9 150.9 %all-to-all-start = ((bf16[8,2,16,2048]{3,2,1,0:T(8,128)(2,1)}), bf16[8,2,16,2048]{3,2,1,0:T(8,128)(2,1)S(1)}, u32[]{:S(2)}, u32[]{:S(2)}) async-start(bf16[8,2,16,2048]{3,2,1,0:T(8,128)(2,1)} %bitcast.2), calls=%async_computation | async-start | bytes 2097152 | tf_op jit(solution)/shard_map/all_to_all | solution.py:48
  528.2 1.3 copy-start
Sparse Core Ops, SparseCore 0:
  8.9 60.9 all-gather.5
  72.1 124.9 all-gather.7
  199.2 123.1 all-gather.9
  323.7 32.6 all-gather.11
  358.4 131.8 all-gather.13
where the time goes:
time: 550 us; the launch traced here: 549 us
  waiting for transfers between devices  439 us (80%)
  matrix products  50.1 us (9%)
  local copies, waits for them, and re-layouts  39.1 us (7%)
  between operations  13.3 us (2%)
    all_gather x1, waiting for transfers between devices, body(): lax.all_gather(query_weight, 'crop', axis=0, tiled=True)  134 us
    all_gather x1, waiting for transfers between devices, body(): keys_full = add_one(lax.all_gather(key_weight, 'crop', axis=0, tiled=True))  127 us
    all_gather x1, waiting for transfers between devices, body(): lax.all_gather(value_weight, 'crop', axis=0, tiled=True)  112 us
    all_gather x1, waiting for transfers between devices, body(): tokens_all = lax.all_gather(crop_tokens, 'head', axis=1, tiled=True)  59.6 us
    dot_general x3, matrix products, add_rows(): return jnp.dot(left, piece, preferred_element_type=jnp.float32)  36.6 us
    slice x2, local copies, waits for them, and re-layouts, body(): keys_row = listed[:, :, :width].reshape(rows_here, NB * CT, heads_here, HD)  12.4 us
  transfers between devices with their start and end apart: 6, of which 5 were waited for; matrix products, arithmetic and copies ran while one was open for 9% of the time, Pallas kernels for 0%

commit v1 on v0

--- a/solution.py
+++ b/solution.py
@@ -33,7 +33,12 @@
         jnp.bfloat16
     )
     picks = fetch_slots[0]
-    tokens_all = lax.all_gather(crop_tokens, "head", axis=1, tiled=True)
+    ring = [crop_tokens]
+    for hop in range(3):
+        ring.append(lax.ppermute(ring[-1], "head", [(dev, (dev + 1) % 4) for dev in range(4)]))
+    tokens_all = jnp.roll(
+        jnp.concatenate(ring[::-1], axis=1), (lax.axis_index("head") + 1) * ring[0].shape[1], axis=1
+    )
 
     def add_one(piece):
         return add_rows(tokens_all, piece)

time: 550 us -> 490 us (0.89)
  waiting for transfers between devices: 439 us -> 360 us
  local copies, waits for them, and re-layouts: 39.1 us -> 57.6 us
    all_gather x1, waiting for transfers between devices: 127 us -> 31.6 us  [body(): keys_full = add_one(lax.all_gather(key_weight, 'crop', axis=0, tiled=True))]
    ppermute x0 -> x3, waiting for transfers between devices: none -> 76.8 us  [body(): lax.ppermute(ring[-1], 'head', [(dev, (dev + 1) % 4) for dev in range(4)])]
    all_gather x1 -> x0, waiting for transfers between devices: 59.6 us -> none  [body(): tokens_all = lax.all_gather(crop_tokens, 'head', axis=1, tiled=True)]
    unnamed x10 -> x19, local copies, waits for them, and re-layouts: 2.86 us -> 19.9 us
  transfers between devices with their start and end apart: 6 -> 8, of which waited for: 5 -> 7; matrix products, arithmetic and copies ran while one was open for 9% -> 14% of each run, Pallas kernels for 0% -> 0%
where the time goes in v1:
time: 490 us; the launch traced here: 489 us
  waiting for transfers between devices  360 us (73%)
  local copies, waits for them, and re-layouts  57.6 us (12%)
  matrix products  50.1 us (10%)
  between operations  13.3 us (3%)
    all_gather x1, waiting for transfers between devices, body(): lax.all_gather(query_weight, 'crop', axis=0, tiled=True)  134 us
    all_gather x1, waiting for transfers between devices, body(): lax.all_gather(value_weight, 'crop', axis=0, tiled=True)  112 us
    ppermute x3, waiting for transfers between devices, body(): lax.ppermute(ring[-1], 'head', [(dev, (dev + 1) % 4) for dev in range(4)])  76.8 us
    dot_general x3, matrix products, add_rows(): return jnp.dot(left, piece, preferred_element_type=jnp.float32)  36.7 us
    all_gather x1, waiting for transfers between devices, body(): keys_full = add_one(lax.all_gather(key_weight, 'crop', axis=0, tiled=True))  31.6 us
    unnamed x19, local copies, waits for them, and re-layouts  19.9 us
    slice x2, local copies, waits for them, and re-layouts, body(): keys_row = listed[:, :, :width].reshape(rows_here, NB * CT, heads_here, HD)  12.4 us
    dot_general x1, matrix products, body(): jnp.einsum('rhgk,rkhe->rghe', weights, vals_row, preferred_element_type=j...  10.1 us
  transfers between devices with their start and end apart: 8, of which 7 were waited for; matrix products, arithmetic and copies ran while one was open for 14% of the time, Pallas kernels for 0%

profile of v1, /device:TPU:0, one launch (start us, length us, event | category | flops | bytes accessed | tf_op | source)
XLA Modules:
  0.0 489.1 jit_solution(3052027532606891487)
XLA Ops:
  9.8 25.9 %collective-permute-done = bf16[1024,1024]{1,0:T(8,128)(2,1)S(1)} collective-permute-done((bf16[1024,1024]{1,0:T(8,128)(2,1)}, bf16[1024,1024]{1,0:T(8,128)(2,1)S(1)}, u32[]{:S(2)}, u32[]{:S(2)}) %collective-permute-start) | collective-permute-done | bytes 2097184 | tf_op jit(solution)/shard_map/ppermute | solution.py:38
  35.7 25.5 %collective-permute-done.1 = bf16[1024,1024]{1,0:T(8,128)(2,1)} collective-permute-done((bf16[1024,1024]{1,0:T(8,128)(2,1)S(1)}, bf16[1024,1024]{1,0:T(8,128)(2,1)}, u32[]{:S(2)}, u32[]{:S(2)}) %collective-permute-start.1) | collective-permute-done | bytes 2097184 | tf_op jit(solution)/shard_map/ppermute | solution.py:38
  61.6 25.4 %collective-permute-done.2 = bf16[1024,1024]{1,0:T(8,128)(2,1)} collective-permute-done((bf16[1024,1024]{1,0:T(8,128)(2,1)}, bf16[1024,1024]{1,0:T(8,128)(2,1)}, u32[]{:S(2)}, u32[]{:S(2)}) %collective-permute-start.2) | collective-permute-done | bytes 2097184 | tf_op jit(solution)/shard_map/ppermute | solution.py:38
  87.0 3.1 constant_dynamic-update-slice_fusion.7
  90.1 3.3 constant_dynamic-update-slice_fusion.6
  96.4 3.1 constant_dynamic-update-slice_fusion.3
  99.5 3.1 constant_dynamic-update-slice_fusion.2
  105.6 31.6 %all-gather.5.cloned.1.call-done = bf16[4096,1024]{1,0:T(8,128)(2,1)} async-done(((bf16[512,1024]{1,0:T(8,128)(2,1)}), bf16[4096,1024]{1,0:T(8,128)(2,1)}) %all-gather.5.cloned.1.call-update) | async-done | bytes 8388624 | tf_op jit(solution)/shard_map/all_gather | solution.py:46
  137.2 13.8 %fusion.5 = bf16[1024,1024]{0,1:T(8,128)(2,1)S(1)} fusion(bf16[4096,1024]{1,0:T(8,128)(2,1)} %all-gather.5.cloned.1.call-done, bf16[1024,8192]{1,0:T(8,128)(2,1)} %constant_dynamic-update-slice_fusion, s32[]{:T(128)S(6)} %select_n.40), kind=kOutput, calls=%fused_computation.11 | convolution fusion | flops 8590983168 | bytes 18874372 | tf_op jit(solution)/shard_map/dot_general | solution.py:14
  150.9 111.6 %all-gather.7.cloned.1.call-done = bf16[4096,1024]{1,0:T(8,128)(2,1)} async-done(((bf16[512,1024]{1,0:T(8,128)(2,1)}), bf16[4096,1024]{1,0:T(8,128)(2,1)}) %all-gather.7.cloned.1.call-update) | async-done | bytes 8388624 | tf_op jit(solution)/shard_map/all_gather | solution.py:47
  262.5 13.8 %fusion.8 = bf16[1024,1024]{0,1:T(8,128)(2,1)S(1)} fusion(bf16[4096,1024]{1,0:T(8,128)(2,1)} %all-gather.7.cloned.1.call-done, bf16[1024,8192]{1,0:T(8,128)(2,1)} %constant_dynamic-update-slice_fusion, s32[]{:T(128)S(6)} %select_n.40), kind=kOutput, calls=%fused_computation.12 | convolution fusion | flops 8590983168 | bytes 18874372 | tf_op jit(solution)/shard_map/dot_general | solution.py:14
  276.3 2.4 pad_maximum_fusion
  278.7 6.5 %copy.12 = bf16[1024,2048]{1,0:T(8,128)(2,1)} copy(bf16[1024,2048]{0,1:T(8,128)(2,1)} %pad_maximum_fusion) | data formatting | bytes 8388608 | tf_op jit(solution)/shard_map/concatenate | solution.py:48
  285.2 3.8 gather_fusion
  289.0 3.7 all-to-all-start
  292.8 3.9 all-gather.9.cloned.1.call-done
  296.8 133.6 %all-gather.11.cloned.1.call-done = bf16[4096,1024]{1,0:T(8,128)(2,1)} async-done(((bf16[512,1024]{1,0:T(8,128)(2,1)}), bf16[4096,1024]{1,0:T(8,128)(2,1)}) %all-gather.11.cloned.1.call-update) | async-done | bytes 8388624 | tf_op jit(solution)/shard_map/all_gather | solution.py:32
  430.4 9.1 %fusion.13 = bf16[64,8,8,128]{3,1,2,0:T(8,128)(2,1)S(1)} fusion(bf16[512,4096]{1,0:T(8,128)(2,1)} %all-gather.9.cloned.1.call-done, bf16[4096,1024]{1,0:T(8,128)(2,1)} %all-gather.11.cloned.1.call-done), kind=kOutput, calls=%fused_computation.17 | convolution fusion | flops 4295491584 | bytes 13631488 | tf_op jit(solution)/shard_map/dot_general | solution.py:14
  439.9 6.2 %gather_fusion.1 = bf16[128,16,2048]{2,1,0:T(8,128)(2,1)} fusion(bf16[16,16,2048]{2,1,0:T(8,128)(2,1)S(1)} %bitcast.27, s32[1024]{0:T(1024)S(1)} %pad_clamp_fusion), kind=kCustom, calls=%fused_computation.1 | custom fusion | bytes 16777728 | tf_op jit(solution)/shard_map/gather | solution.py:55
  446.1 6.0 %fusion.29 = (bf16[16,128,1024]{2,1,0:T(8,128)(2,1)}, bf16[16,128,1024]{2,1,0:T(8,128)(2,1)}) fusion(bf16[16,128,2048]{2,1,0:T(8,128)(2,1)} %bitcast.28), kind=kLoop, calls=%fused_computation.49 | loop fusion | bytes 16777216 | tf_op jit(solution)/shard_map/slice | solution.py:56
  452.1 6.4 %copy.16 = bf16[16,128,1024]{1,2,0:T(8,128)(2,1)} copy(bf16[16,128,1024]{2,1,0:T(8,128)(2,1)} %get-tuple-element.5) | data formatting | bytes 8388608 | tf_op jit(solution)/shard_map/slice | solution.py:56
  458.5 6.4 %copy.15 = bf16[16,128,1024]{1,2,0:T(8,128)(2,1)} copy(bf16[16,128,1024]{2,1,0:T(8,128)(2,1)} %get-tuple-element.6) | data formatting | bytes 8388608 | tf_op jit(solution)/shard_map/slice | solution.py:57
  464.9 3.4 fusion.14
  470.8 10.1 %fusion.12 = bf16[16,32,8,128]{3,1,2,0:T(8,128)(2,1)S(1)} fusion(bf16[16,128,8,128]{1,3,2,0:T(8,128)(2,1)} %bitcast.32, f32[16,8,32]{2,1,0:T(8,128)S(1)} %fusion.30, f32[16,8,32,128]{3,2,1,0:T(8,128)} %copy-done.1, pred[16,128]{1,0:T(8,128)(4,1)S(1)} %broadcast_compare_fusion), kind=kOutput, calls=%fused_computation.16 | convolution fusion | flops 137367680 | bytes 7358464 | tf_op jit(solution)/shard_map/rhgk,rkhe->rghe/dot_general | solution.py:69
  (40 shorter events, 14.2 us)
Async XLA Ops:
  6.5 54.7 %copy-start.3 = (s32[1,8,2]{1,2,0:T(2,128)S(1)}, s32[1,8,2]{1,2,0:T(2,128)}, u32[]{:S(2)}) copy-start(s32[1,8,2]{1,2,0:T(2,128)} %param.13) | copy-start | bytes 196
  6.5 54.9 %copy-start.2 = (s32[16,8]{0,1:T(8,128)S(1)}, s32[16,8]{0,1:T(8,128)}, u32[]{:S(2)}) copy-start(s32[16,8]{0,1:T(8,128)} %param.14) | copy-start | bytes 1540
  6.5 130.6 %all-gather.5.cloned.1.call-start = ((), (), s32[]{:S(2)}) async-start(), calls=%async_computation.1 | async-start | bytes 9437184 | tf_op jit(solution)/shard_map/all_gather | solution.py:46
  7.3 255.3 %all-gather.7.cloned.1.call-start = ((), (), s32[]{:S(2)}) async-start(), calls=%async_computation.2 | async-start | bytes 9437184 | tf_op jit(solution)/shard_map/all_gather | solution.py:47
  8.0 288.8 %all-gather.9.cloned.1.call-start = ((), (), s32[]{:S(2)}) async-start(), calls=%async_computation.3 | async-start | bytes 5242880 | tf_op jit(solution)/shard_map/all_gather | solution.py:31
  8.7 421.7 %all-gather.11.cloned.1.call-start = ((), (), s32[]{:S(2)}) async-start(), calls=%async_computation.4 | async-start | bytes 9437184 | tf_op jit(solution)/shard_map/all_gather | solution.py:32
  9.3 26.4 %collective-permute-start = (bf16[1024,1024]{1,0:T(8,128)(2,1)}, bf16[1024,1024]{1,0:T(8,128)(2,1)S(1)}, u32[]{:S(2)}, u32[]{:S(2)}) collective-permute-start(bf16[1024,1024]{1,0:T(8,128)(2,1)} %param.9), channel_id=1, source_target_pairs={{0,1},{1,2},{2,3},{3,0},{4,5},{5,6},{6,7},{7,4},{8,9},{9,10},{10,1... | collective-permute-start | bytes 6291464 | tf_op jit(solution)/shard_map/ppermute | solution.py:38
  35.7 25.6 %collective-permute-start.1 = (bf16[1024,1024]{1,0:T(8,128)(2,1)S(1)}, bf16[1024,1024]{1,0:T(8,128)(2,1)}, u32[]{:S(2)}, u32[]{:S(2)}) collective-permute-start(bf16[1024,1024]{1,0:T(8,128)(2,1)S(1)} %collective-permute-done), channel_id=1, source_target_pairs={{0,1},{1,2},{2,3},{3,0},{4,5},{5,6},{6,7},{7,4},{8,9},{9,10},{10,1... | collective-permute-start | bytes 6291464 | tf_op jit(solution)/shard_map/ppermute | solution.py:38
  61.2 25.8 %collective-permute-start.2 = (bf16[1024,1024]{1,0:T(8,128)(2,1)}, bf16[1024,1024]{1,0:T(8,128)(2,1)}, u32[]{:S(2)}, u32[]{:S(2)}) collective-permute-start(bf16[1024,1024]{1,0:T(8,128)(2,1)} %collective-permute-done.1), channel_id=1, source_target_pairs={{0,1},{1,2},{2,3},{3,0},{4,5},{5,6},{6,7},{7,4},{8,9},{9,10},{10,1... | collective-permute-start | bytes 6291464 | tf_op jit(solution)/shard_map/ppermute | solution.py:38
  90.1 4.8 copy-start
  285.2 7.5 %copy-start.4 = (s32[16]{0:T(128)S(1)}, s32[16]{0:T(128)}, u32[]{:S(2)}) copy-start(s32[16]{0:T(128)} %param.15) | copy-start | bytes 196
  289.0 150.8 %all-to-all-start = ((bf16[8,2,16,2048]{3,2,1,0:T(8,128)(2,1)}), bf16[8,2,16,2048]{3,2,1,0:T(8,128)(2,1)S(1)}, u32[]{:S(2)}, u32[]{:S(2)}) async-start(bf16[8,2,16,2048]{3,2,1,0:T(8,128)(2,1)} %bitcast.2), calls=%async_computation | async-start | bytes 2097152 | tf_op jit(solution)/shard_map/all_to_all | solution.py:53
  468.3 1.3 copy-start.1
Sparse Core Ops, SparseCore 0:
  9.5 127.6 all-gather.4
  139.3 123.1 all-gather.6
  264.1 32.6 all-gather.8
  298.8 131.6 all-gather.10
